TPU v7x, 32 devices: a whole 2x2x4 slice. The times are simulated.
32 devices in a mesh: groups: 2 (over y), tensor: 4 (over z), seq: 2 (over x), load: 2 (over core).
Axes of the slice: x: 2, y: 2, z: 4, core: 2. Of those that a mesh axis runs over, the one named last changes fastest.
Arguments:
- tokens: bfloat16 [1024, 16384], P(('groups', 'tensor'), ('seq', 'load')), parts along dimension 0, may hold values from -21 to 21
- weight_query: bfloat16 [16384, 16384], P(('seq', 'load'), 'tensor'), may hold values from -0.046875 to 0.046875
- weight_keyval: bfloat16 [16384, 2048], P(('seq', 'load'), 'tensor'), may hold values from -0.046875 to 0.046875
- down_query: bfloat16 [16384, 1024], P(('seq', 'load'), ('groups', 'tensor')), parts along dimension 1, may hold values from -0.046875 to 0.046875
- down_keyval: bfloat16 [16384, 1024], P(('seq', 'load'), ('groups', 'tensor')), parts along dimension 1, may hold values from -0.046875 to 0.046875
- up_query: bfloat16 [1024, 16384], P(('groups', 'load'), 'tensor'), parts along dimension 0, may hold values from -0.5 to 0.5
- up_keyval: bfloat16 [1024, 2048], P(('groups', 'load'), 'tensor'), parts along dimension 0, may hold values from -0.5 to 0.5
- adapter_rank: int32 [8], P('groups'), parts along dimension 0, may hold values from 8 to 128, as said below
- token_lengths: int32 [8], P('groups'), parts along dimension 0, may hold values from 1 to 384, 512 in all
- adapter_slot: int32 [8], P('groups'), parts along dimension 0, may hold values from 0 to 3, each once
Outputs:
- context: bfloat16 [1024, 16384], P(('groups', 'seq', 'load'), 'tensor'), parts along dimension 0
- kv_cache: bfloat16 [1024, 2048], P(('groups', 'seq', 'load'), 'tensor'), parts along dimension 0
There are 2 independent parts, one for each index of `groups`. A program takes and returns all parts, laid end to end along the dimension named above; an argument that names none is the same for every part. Nothing has to cross between parts.
Inputs may be any that keep to these rules, and one draw needn't show every extreme that they name: `adapter_rank`: each rank is a power of two; some tenant has rank 128 and some has rank 8. `token_lengths`: the lengths sum to 512; some tenant has exactly 384 tokens. `adapter_slot`: each slot belongs to exactly one tenant.
All inputs are finite; a program needn't handle non-finite values.
Results may differ from a plain program's by a relative error of at most 0.0025.
The roundings to bfloat16 on the way count: a program that leaves them out, or rounds other values in their place, can miss the bound.
Values may be sent and summed in bfloat16 or wider, within the bound.
No kernel may reach another device: no remote copies, remote signals or barrier semaphores. Data moves between devices by JAX's collectives and lax.ppermute only.
A program may use at most 128 MiB of HBM per device.

v0:
```python
import math
import jax
import jax.numpy as jnp
from jax import lax
from jax.sharding import PartitionSpec as P

HEADS = 128
KV_HEADS = 8
HEAD_DIM = 128
TENANTS = 4
ROPE_BASE = 500000.0
ADAPTER_ALPHA = 8.0


def product(left, right):
    return jnp.dot(left, right, preferred_element_type=jnp.float32)


def rotate_pairs(values, position, first_col):
    cols = values.shape[1]
    width = HEAD_DIM if cols % HEAD_DIM == 0 else cols
    col = jnp.arange(width, dtype=jnp.int32)
    pair_col = first_col + col - col % 2
    within = pair_col % HEAD_DIM // 2
    frequency = jnp.exp(-(2.0 * within.astype(jnp.float32) / HEAD_DIM) * math.log(ROPE_BASE))
    angles = position.astype(jnp.float32)[:, None] * frequency[None, :]
    cosine = jnp.cos(angles)
    sine_angle = jnp.sin(angles)
    signed_sine = jnp.where((col % 2 == 0)[None, :], -sine_angle, sine_angle)
    cosine, signed_sine = lax.optimization_barrier((cosine, signed_sine))
    cosine = jnp.tile(cosine, (1, cols // width))
    signed_sine = jnp.tile(signed_sine, (1, cols // width))
    is_even = (jnp.arange(cols, dtype=jnp.int32) % 2 == 0)[None, :]
    partner = jnp.where(is_even, jnp.roll(values, -1, axis=1), jnp.roll(values, 1, axis=1))
    return values * cosine + partner * signed_sine


def tenant_table(token_ids, adapter_rank, token_lengths, adapter_slot):
    segment_ends = jnp.cumsum(token_lengths)
    begins = segment_ends - token_lengths
    owned_rows = (token_ids[:, None] >= begins[None, :]) & (
        token_ids[:, None] < segment_ends[None, :]
    )
    zero_int = jnp.zeros((), jnp.int32)
    own_rank = jnp.sum(jnp.where(owned_rows, adapter_rank[None, :], zero_int), axis=1)
    own_slot = jnp.sum(jnp.where(owned_rows, adapter_slot[None, :], zero_int), axis=1)
    own_first = jnp.sum(jnp.where(owned_rows, begins[None, :], zero_int), axis=1)
    slot_hot = own_slot[:, None] == jnp.arange(TENANTS, dtype=jnp.int32)[None, :]
    return (own_rank, own_first, slot_hot)


def select_slot(down_values, slot_hot):
    shaped = down_values.reshape(down_values.shape[0], -1, TENANTS)
    return jnp.sum(jnp.where(slot_hot[:, None, :], shaped, 0.0), axis=2)


def scale_ranks(picked, own_rank, first_rank):
    rank_index = first_rank + jnp.arange(picked.shape[1], dtype=jnp.int32)
    keep_mask = rank_index[None, :] < own_rank[:, None]
    factor = ADAPTER_ALPHA / jnp.sqrt(own_rank.astype(jnp.float32))
    return jnp.where(keep_mask, picked * factor[:, None], 0.0).astype(jnp.bfloat16)


def widen_slots(low_values, slot_hot):
    wide_rows = jnp.where(
        slot_hot[:, None, :], low_values[:, :, None], jnp.zeros((), low_values.dtype)
    )
    return wide_rows.reshape(low_values.shape[0], -1)


def ring_reduce_scatter(blocks, axis):
    count = lax.axis_size(axis)
    me = lax.axis_index(axis)
    if count == 1:
        return blocks[0]
    shift = [(i, (i + 1) % count) for i in range(count)]

    def pick(step):
        return lax.dynamic_index_in_dim(blocks, (me - 1 - step) % count, 0, keepdims=False)

    total = pick(0)
    for step in range(1, count):
        total = lax.ppermute(total, axis, shift) + pick(step)
    return total


def shards(
    tokens,
    weight_query,
    weight_keyval,
    down_query,
    down_keyval,
    up_query,
    up_keyval,
    adapter_rank,
    token_lengths,
    adapter_slot,
):
    tensor_count = lax.axis_size("tensor")
    block_count = lax.axis_size(("seq", "load"))
    tensor_index = lax.axis_index("tensor")
    block_index = lax.axis_index(("seq", "load"))
    query_cols = weight_query.shape[1]
    keyval_cols = weight_keyval.shape[1]
    rank_share = down_query.shape[1] // TENANTS
    block_rows = tokens.shape[0] * tensor_count // block_count
    up_query_all = lax.all_gather(up_query, "load", axis=0, tiled=True)
    up_keyval_all = lax.all_gather(up_keyval, "load", axis=0, tiled=True)
    ring = tensor_count
    chunk = tokens.shape[0]
    small_cols = keyval_cols + 2 * rank_share
    small_terms = jnp.zeros((ring, chunk, small_cols), jnp.float32)
    query_terms = jnp.zeros((ring, chunk, query_cols), jnp.float32)
    shift = [(i, (i + 1) % ring) for i in range(ring)]
    held = tokens
    for step in range(ring):
        following = lax.ppermute(held, "tensor", shift) if step < ring - 1 else None
        owner = (tensor_index - step) % ring
        block_ids = owner * chunk + jnp.arange(chunk, dtype=jnp.int32)
        _, _, block_hot = tenant_table(block_ids, adapter_rank, token_lengths, adapter_slot)
        small_block = jnp.concatenate(
            [
                product(held, weight_keyval),
                select_slot(product(held, down_query), block_hot),
                select_slot(product(held, down_keyval), block_hot),
            ],
            axis=1,
        )
        small_terms = lax.dynamic_update_slice_in_dim(small_terms, small_block[None], owner, 0)
        if step == 0 and ring > 2:
            first_block, first_owner = (held, owner)
        elif step == 1 and ring > 2:
            pair = product(jnp.concatenate([first_block, held], axis=0), weight_query)
            query_terms = lax.dynamic_update_slice_in_dim(
                query_terms, pair[:chunk][None], first_owner, 0
            )
            query_terms = lax.dynamic_update_slice_in_dim(query_terms, pair[chunk:][None], owner, 0)
        else:
            query_terms = lax.dynamic_update_slice_in_dim(
                query_terms, product(held, weight_query)[None], owner, 0
            )
        if following is not None:
            if step == 0 and ring > 2:
                following, small_terms, first_block = lax.optimization_barrier(
                    (following, small_terms, first_block)
                )
            else:
                following, small_terms, query_terms = lax.optimization_barrier(
                    (following, small_terms, query_terms)
                )
        held = following
    seq_count = lax.axis_size("seq")
    load_count = lax.axis_size("load")
    by_core = small_terms.reshape(seq_count, load_count, block_rows, -1)
    per_core = ring_reduce_scatter(jnp.moveaxis(by_core, 1, 0), "load")
    small_summed = ring_reduce_scatter(per_core, "seq")
    query_summed = lax.psum_scatter(
        query_terms.reshape(ring * chunk, -1), ("seq", "load"), scatter_dimension=0, tiled=True
    )
    token_ids = block_index * block_rows + jnp.arange(block_rows, dtype=jnp.int32)
    own_rank, own_first, slot_hot = tenant_table(
        token_ids, adapter_rank, token_lengths, adapter_slot
    )
    position = token_ids - own_first
    first_rank = tensor_index * rank_share
    low_query = scale_ranks(
        small_summed[:, keyval_cols : keyval_cols + rank_share], own_rank, first_rank
    )
    low_keyval = scale_ranks(small_summed[:, keyval_cols + rank_share :], own_rank, first_rank)
    low_both = lax.all_gather(jnp.concatenate([low_query, low_keyval], axis=1), "tensor", axis=1)
    full_query = low_both[:, :, :rank_share].reshape(block_rows, -1)
    full_keyval = low_both[:, :, rank_share:].reshape(block_rows, -1)
    wide_query = widen_slots(full_query, slot_hot)
    wide_keyval = widen_slots(full_keyval, slot_hot)
    delta_keyval = product(wide_keyval, up_keyval_all)
    keyval = small_summed[:, :keyval_cols] + delta_keyval
    kv_first_col = tensor_index * keyval_cols
    is_key = kv_first_col + jnp.arange(keyval_cols, dtype=jnp.int32) < KV_HEADS * HEAD_DIM
    kv_local = jnp.where(
        is_key[None, :], rotate_pairs(keyval, position, kv_first_col), keyval
    ).astype(jnp.bfloat16)
    kv_all = lax.all_gather(kv_local, "tensor", axis=1, tiled=True)
    heads_here = query_cols // HEAD_DIM
    group_size = HEADS // KV_HEADS
    kv_here = max(heads_here // group_size, 1)
    per_kv = heads_here // kv_here
    kv_first = tensor_index * heads_here // group_size
    key_cols = KV_HEADS * HEAD_DIM
    key_heads = lax.dynamic_slice_in_dim(
        kv_all, kv_first * HEAD_DIM, kv_here * HEAD_DIM, 1
    ).reshape(block_rows, kv_here, HEAD_DIM)
    value_heads = lax.dynamic_slice_in_dim(
        kv_all, key_cols + kv_first * HEAD_DIM, kv_here * HEAD_DIM, 1
    ).reshape(block_rows, kv_here, HEAD_DIM)
    both_heads = lax.all_gather(
        jnp.concatenate([key_heads, value_heads], axis=1), ("seq", "load"), axis=0, tiled=True
    )
    piece_keys = both_heads[:, :kv_here]
    piece_values = both_heads[:, kv_here:]
    delta_query = lax.optimization_barrier(product(wide_query, up_query_all))
    query_rows = rotate_pairs(
        query_summed + delta_query, position, tensor_index * query_cols
    ).astype(jnp.bfloat16)
    grouped = query_rows.reshape(block_rows, kv_here, per_kv, HEAD_DIM)
    key_ids = jnp.arange(piece_keys.shape[0], dtype=jnp.int32)
    visible = (key_ids[None, :] >= own_first[:, None]) & (key_ids[None, :] <= token_ids[:, None])
    scores = jnp.einsum(
        "qghd,kgd->ghqk", grouped, piece_keys, preferred_element_type=jnp.float32
    ) / math.sqrt(HEAD_DIM)
    scores = jnp.where(visible, scores, -1e30)
    row_top = jnp.max(scores, axis=3)
    exp_scores = jnp.where(visible, jnp.exp(scores - row_top[..., None]), 0.0)
    row_total = jnp.sum(exp_scores, axis=3)
    accumulated = jnp.einsum(
        "ghqk,kgd->ghqd",
        exp_scores.astype(jnp.bfloat16),
        piece_values,
        preferred_element_type=jnp.float32,
    )
    context = (accumulated / row_total[..., None]).astype(jnp.bfloat16)
    context = jnp.transpose(context, (2, 0, 1, 3)).reshape(block_rows, query_cols)
    return (context, kv_local)


def solution(mesh):
    placed = (
        P(("groups", "tensor"), ("seq", "load")),
        P(("seq", "load"), "tensor"),
        P(("seq", "load"), "tensor"),
        P(("seq", "load"), ("groups", "tensor")),
        P(("seq", "load"), ("groups", "tensor")),
        P(("groups", "load"), "tensor"),
        P(("groups", "load"), "tensor"),
        P("groups"),
        P("groups"),
        P("groups"),
    )
    return jax.shard_map(
        shards,
        mesh=mesh,
        in_specs=placed,
        out_specs=(P(("groups", "seq", "load"), "tensor"), P(("groups", "seq", "load"), "tensor")),
        check_vma=False,
    )
```

profile of v0, /device:TPU:0, one launch (start us, length us, event | category | flops | bytes accessed | tf_op | source)
XLA Modules:
  0.0 206.6 jit_solution(1513930682166711280)
XLA Ops:
  8.1 3.1 %collective-permute-start = (bf16[128,4096]{1,0:T(8,128)(2,1)}, bf16[128,4096]{1,0:T(8,128)(2,1)}, u32[]{:S(2)}, u32[]{:S(2)}) collective-permute-start(bf16[128,4096]{1,0:T(8,128)(2,1)} %param.10), channel_id=1, source_target_pairs={{0,4},{4,8},{8,12},{12,0},{1,5},{5,9},{9,13},{13,1},{2,6},{6,10},{... | collective-permute-start | bytes 3145736 | tf_op jit(solution)/shard_map/ppermute | solution.py:117
  11.4 0.8 reduce-window.8
  12.2 0.7 bitcast_subtract_fusion
  12.9 1.7 fusion.49
  14.7 0.5 fusion.50
  15.2 0.6 select_reduce_fusion.8
  16.1 2.9 %fusion.48 = f32[128,512]{1,0:T(8,128)S(1)} fusion(bf16[128,4096]{1,0:T(8,128)(2,1)S(1)} %copy-done.5, bf16[4096,512]{1,0:T(8,128)(2,1)} %param.12), kind=kOutput, calls=%fused_computation.146 | convolution fusion | flops 536870912 | bytes 5505024 | tf_op jit(solution)/shard_map/dot_general | solution.py:16
  19.2 0.1 copy.69
  19.3 1.1 broadcast_in_dim.269
  20.4 0.7 constant_dynamic-update-slice_fusion.3
  21.2 15.5 %collective-permute-done = bf16[128,4096]{1,0:T(8,128)(2,1)} collective-permute-done((bf16[128,4096]{1,0:T(8,128)(2,1)}, bf16[128,4096]{1,0:T(8,128)(2,1)}, u32[]{:S(2)}, u32[]{:S(2)}) %collective-permute-start) | collective-permute-done | bytes 1048608 | tf_op jit(solution)/shard_map/ppermute | solution.py:117
  36.7 1.7 fusion.52
  38.4 1.7 fusion.53
  40.2 2.8 %fusion.51 = f32[128,512]{1,0:T(8,128)} fusion(bf16[128,4096]{1,0:T(8,128)(2,1)} %collective-permute-done, bf16[4096,512]{1,0:T(8,128)(2,1)S(1)} %copy-done.1), kind=kOutput, calls=%fused_computation.149 | convolution fusion | flops 536870912 | bytes 5505024 | tf_op jit(solution)/shard_map/dot_general | solution.py:16
  43.2 0.7 copy.71
  43.9 1.1 maximum_bitcast_fusion.1
  45.0 0.9 copy.72
  45.9 15.3 %fusion.13 = f32[256,4096]{1,0:T(8,128)S(1)} fusion(bf16[4096,4096]{1,0:T(8,128)(2,1)} %param.11, bf16[128,4096]{1,0:T(8,128)(2,1)} %collective-permute-done, bf16[128,4096]{1,0:T(8,128)(2,1)S(1)} %copy-done.6), kind=kOutput, calls=%fused_computation.21 | convolution fusion | flops 8594128896 | bytes 39845888 | tf_op jit(solution)/shard_map/dot_general | solution.py:16
  61.2 4.3 %broadcast_in_dim.276 = f32[4,128,4096]{2,1,0:T(8,128)} broadcast(f32[]{:T(128)} %constant.193.clone.1), dimensions={} | broadcast | bytes 8388612 | tf_op jit(solution)/shard_map/broadcast_in_dim | solution.py:113
  65.5 1.5 fusion.12
  67.0 0.7 constant_dynamic-update-slice_fusion.2
  67.8 1.5 fusion.11
  69.4 1.2 collective-permute-start.2
  70.5 14.2 %fusion.3 = f32[4,128,4096]{2,1,0:T(8,128)} fusion(f32[4,128,4096]{2,1,0:T(8,128)} %fusion.11, s32[]{:T(128)S(6)} %select_n.264, bf16[128,4096]{1,0:T(8,128)(2,1)S(1)} %collective-permute-done.1, bf16[4096,4096]{1,0:T(8,128)(2,1)} %param.11), kind=kOutput, calls=%fused_computation.7 | convolution fusion | flops 4294967296 | bytes 36700164 | tf_op jit(solution)/shard_map/dot_general | solution.py:16
  84.8 0.5 fusion.55
  85.3 0.5 fusion.56
  86.1 0.7 copy.74
  86.8 2.9 %fusion.54 = f32[128,512]{1,0:T(8,128)S(1)} fusion(bf16[128,4096]{1,0:T(8,128)(2,1)S(1)} %collective-permute-done.1, bf16[4096,512]{1,0:T(8,128)(2,1)} %param.12), kind=kOutput, calls=%fused_computation.152 | convolution fusion | flops 536870912 | bytes 5505024 | tf_op jit(solution)/shard_map/dot_general | solution.py:16
  89.8 0.9 copy.75
  90.7 1.7 constant_dynamic-update-slice_fusion.1
  92.4 3.0 %collective-permute-done.2 = bf16[128,4096]{1,0:T(8,128)(2,1)S(1)} collective-permute-done((bf16[128,4096]{1,0:T(8,128)(2,1)S(1)}, bf16[128,4096]{1,0:T(8,128)(2,1)S(1)}, u32[]{:S(2)}, u32[]{:S(2)}) %collective-permute-start.2) | collective-permute-done | bytes 1048608 | tf_op jit(solution)/shard_map/ppermute | solution.py:117
  95.4 14.2 %fusion.2 = f32[4,128,4096]{2,1,0:T(8,128)} fusion(f32[4,128,4096]{2,1,0:T(8,128)} %fusion.3, s32[]{:T(128)S(6)} %select_n.269, bf16[128,4096]{1,0:T(8,128)(2,1)S(1)} %collective-permute-done.2, bf16[4096,4096]{1,0:T(8,128)(2,1)} %param.11), kind=kOutput, calls=%fused_computation.5 | convolution fusion | flops 4294967296 | bytes 36700164 | tf_op jit(solution)/shard_map/dot_general | solution.py:16
  109.8 0.5 copy-done.13
  110.3 0.5 fusion.58
  110.9 0.5 fusion.59
  111.7 2.9 %fusion.57 = f32[128,512]{1,0:T(8,128)S(1)} fusion(bf16[128,4096]{1,0:T(8,128)(2,1)S(1)} %collective-permute-done.2, bf16[4096,512]{1,0:T(8,128)(2,1)} %param.12), kind=kOutput, calls=%fused_computation.155 | convolution fusion | flops 536870912 | bytes 5505024 | tf_op jit(solution)/shard_map/dot_general | solution.py:16
  114.8 0.1 copy.78
  114.9 0.7 constant_dynamic-update-slice_fusion
  115.7 1.2 dynamic-slice_bitcast_fusion
  116.9 0.5 negate_select_fusion.1
  117.5 0.5 fusion.33
  118.1 2.6 %all_gather.20 = bf16[512,512]{1,0:T(8,128)(2,1)S(1)} all-gather(bf16[256,512]{1,0:T(8,128)(2,1)S(1)} %copy-done.10), channel_id=1, replica_groups=mesh['groups'=2,'tensor'=4,'seq'=2,'load'=2] {'load'}, dimensions={0}, use_global_device_ids=true | all-gather | bytes 786432 | tf_op jit(solution)/shard_map/all_gather | solution.py:108
  120.7 1.3 bitcast_add_fusion
  122.1 0.2 copy.79
  122.2 1.2 collective-permute-start.4
  123.4 0.7 fusion.26
  124.1 0.2 copy.80
  124.3 7.8 %collective-permute-done.4 = f32[128,576]{1,0:T(8,128)S(1)} collective-permute-done((f32[128,576]{1,0:T(8,128)S(1)}, f32[128,576]{1,0:T(8,128)S(1)}, u32[]{:S(2)}, u32[]{:S(2)}) %collective-permute-start.4) | collective-permute-done | bytes 294944 | tf_op jit(solution)/shard_map/ppermute | solution.py:83
  132.4 13.1 %all-gather = bf16[128,256]{0,1:T(8,128)(2,1)S(1)} all-gather(bf16[128,64]{0,1:T(8,128)(2,1)S(1)} %copy.81), channel_id=2, replica_groups=mesh['groups'=2,'tensor'=4,'seq'=2,'load'=2] {'tensor'}, dimensions={1}, use_global_device_ids=true | all-gather | bytes 81920 | tf_op jit(solution)/shard_map/all_gather | solution.py:170
  145.6 0.1 broadcast_select_fusion.1
  145.7 0.3 slice_add_fusion
  146.3 0.2 fusion.25
  146.5 15.0 %all_gather.21 = bf16[128,2048]{1,0:T(8,128)(2,1)S(1)} all-gather(bf16[128,512]{1,0:T(8,128)(2,1)S(1)} %fusion.25), channel_id=1, replica_groups=mesh['groups'=2,'tensor'=4,'seq'=2,'load'=2] {'tensor'}, dimensions={1}, use_global_device_ids=true | all-gather | bytes 655360 | tf_op jit(solution)/shard_map/all_gather | solution.py:182
  162.1 11.1 %all_gather.22 = bf16[512,4,128]{2,0,1:T(8,128)(2,1)} all-gather(bf16[128,4,128]{2,0,1:T(8,128)(2,1)S(1)} %pad_maximum_fusion), channel_id=1, replica_groups=mesh['groups'=2,'tensor'=4,'seq'=2,'load'=2] {'seq','load'}, dimensions={0}, use_global_device_ids=true | all-gather | bytes 655360 | tf_op jit(solution)/shard_map/all_gather | solution.py:195
  173.2 2.9 %fusion.60 = f32[128,4096]{1,0:T(8,128)S(1)} fusion(bf16[128,512]{0,1:T(8,128)(2,1)S(1)} %bitcast.152, bf16[512,4096]{1,0:T(8,128)(2,1)} %all-gather.3.cloned.1.call-done), kind=kOutput, calls=%fused_computation.158 | convolution fusion | flops 536870912 | bytes 6422528 | tf_op jit(solution)/shard_map/dot_general | solution.py:16
  176.1 7.4 %reduce-scatter.2.cloned.1.call-done = f32[128,4096]{1,0:T(8,128)} async-done(((f32[512,4096]{1,0:T(8,128)}), f32[128,4096]{1,0:T(8,128)}) %reduce-scatter.2.cloned.1.call-update) | async-done | bytes 2097168 | tf_op jit(solution)/shard_map/reduce_scatter | solution.py:157
  183.6 1.8 add.313
  185.4 0.7 fusion.42
  186.5 4.4 %fusion.22 = bf16[16,8,32,128]{3,1,2,0:T(8,128)(2,1)S(1)} fusion(f32[16,8,32,128]{3,2,1,0:T(8,128)S(1)} %bitcast.148, f32[128,4095]{1,0:T(8,128)S(1)} %get-tuple-element.58, f32[128,1]{1,0:T(8,128)S(1)} %get-tuple-element.60, f32[128,1]{1,0:T(8,128)S(1)} %get-tuple-element.59, f32[128,4095]{1,0:T(8,128)S(1)} %get-tuple-element.57, f32[128,4096]{1,0:T(8,128)S(1)} %add.313, ...), kind=kLoop, calls=%fused_computation.30 | loop fusion | flops 3670016 | bytes 11538432
  190.9 0.2 copy.99
  191.1 1.3 fusion.20
  192.4 4.6 %fusion.47 = (f32[2,16,128]{2,1,0:T(8,128)S(1)}, bf16[2,16,128,512]{2,3,1,0:T(8,128)(2,1)S(1)}) fusion(f32[2,512,128,16]{2,1,3,0:T(8,128)S(1)} %fusion.20, pred[128,512]{0,1:T(8,128)(4,1)S(1)} %copy-done.12), kind=kOutput, calls=%fused_computation.145 | output fusion | flops 16777728 | bytes 12664832 | tf_op jit(solution)/shard_map/sub | solution.py:212
  197.0 0.8 fusion.17
  197.8 1.3 copy.89
  (92 shorter events, 3.3 us)
Async XLA Ops:
  8.0 4.9 %copy-start = (bf16[4096,128]{1,0:T(8,128)(2,1)S(1)}, bf16[4096,128]{1,0:T(8,128)(2,1)}, u32[]{:S(2)}) copy-start(bf16[4096,128]{1,0:T(8,128)(2,1)} %param.13) | copy-start | bytes 3145732
  8.0 6.6 %copy-start.5 = (bf16[128,4096]{1,0:T(8,128)(2,1)S(1)}, bf16[128,4096]{1,0:T(8,128)(2,1)}, u32[]{:S(2)}) copy-start(bf16[128,4096]{1,0:T(8,128)(2,1)} %param.10) | copy-start | bytes 3145732
  8.0 6.6 %copy-start.2 = (bf16[4096,128]{1,0:T(8,128)(2,1)S(1)}, bf16[4096,128]{1,0:T(8,128)(2,1)}, u32[]{:S(2)}) copy-start(bf16[4096,128]{1,0:T(8,128)(2,1)} %param.14) | copy-start | bytes 3145732
  8.0 7.2 %copy-start.17 = (s32[4]{0:T(128)S(1)}, s32[4]{0:T(128)}, u32[]{:S(2)}) copy-start(s32[4]{0:T(128)} %param.17) | copy-start | bytes 52
  8.0 7.2 %copy-start.18 = (s32[4]{0:T(128)S(1)}, s32[4]{0:T(128)}, u32[]{:S(2)}) copy-start(s32[4]{0:T(128)} %param.19) | copy-start | bytes 52
  8.1 165.1 %all-gather.3.cloned.1.call-start = ((), (), s32[]{:S(2)}) async-start(), calls=%async_computation.2 | async-start | bytes 6291456 | tf_op jit(solution)/shard_map/all_gather | solution.py:107
  8.1 28.6 %collective-permute-start = (bf16[128,4096]{1,0:T(8,128)(2,1)}, bf16[128,4096]{1,0:T(8,128)(2,1)}, u32[]{:S(2)}, u32[]{:S(2)}) collective-permute-start(bf16[128,4096]{1,0:T(8,128)(2,1)} %param.10), channel_id=1, source_target_pairs={{0,4},{4,8},{8,12},{12,0},{1,5},{5,9},{9,13},{13,1},{2,6},{6,10},{... | collective-permute-start | bytes 3145736 | tf_op jit(solution)/shard_map/ppermute | solution.py:117
  11.2 172.4 %reduce-scatter.2.cloned.1.call-start = ((), (), s32[]{:S(2)}) async-start(), calls=%async_computation.1 | async-start | bytes 10485760 | tf_op jit(solution)/shard_map/reduce_scatter | solution.py:157
  19.3 20.9 %copy-start.1 = (bf16[4096,512]{1,0:T(8,128)(2,1)S(1)}, bf16[4096,512]{1,0:T(8,128)(2,1)}, u32[]{:S(2)}) copy-start(bf16[4096,512]{1,0:T(8,128)(2,1)} %param.12) | copy-start | bytes 12582916
  40.2 5.7 %copy-start.6 = (bf16[128,4096]{1,0:T(8,128)(2,1)S(1)}, bf16[128,4096]{1,0:T(8,128)(2,1)}, u32[]{:S(2)}) copy-start(bf16[128,4096]{1,0:T(8,128)(2,1)} %param.10) | copy-start | bytes 3145732
  43.0 26.4 %collective-permute-start.1 = (bf16[128,4096]{1,0:T(8,128)(2,1)}, bf16[128,4096]{1,0:T(8,128)(2,1)S(1)}, u32[]{:S(2)}, u32[]{:S(2)}) collective-permute-start(bf16[128,4096]{1,0:T(8,128)(2,1)} %collective-permute-done), channel_id=1, source_target_pairs={{0,4},{4,8},{8,12},{12,0},{1,5},{5,9},{9,13},{13,1},{2,6},{6,10},{... | collective-permute-start | bytes 3145736 | tf_op jit(solution)/shard_map/ppermute | solution.py:117
  65.5 1.5 copy-start.8
  69.3 16.0 %copy-start.3 = (bf16[4096,128]{1,0:T(8,128)(2,1)S(1)}, bf16[4096,128]{1,0:T(8,128)(2,1)}, u32[]{:S(2)}) copy-start(bf16[4096,128]{1,0:T(8,128)(2,1)} %param.14) | copy-start | bytes 3145732
  69.4 26.1 %collective-permute-start.2 = (bf16[128,4096]{1,0:T(8,128)(2,1)S(1)}, bf16[128,4096]{1,0:T(8,128)(2,1)S(1)}, u32[]{:S(2)}, u32[]{:S(2)}) collective-permute-start(bf16[128,4096]{1,0:T(8,128)(2,1)S(1)} %collective-permute-done.1), channel_id=1, source_target_pairs={{0,4},{4,8},{8,12},{12,0},{1,5},{5,9},{9,13},{13,1},{2,6},{6,10},{... | collective-permute-start | bytes 3145736 | tf_op jit(solution)/shard_map/ppermute | solution.py:117
  86.8 2.9 %copy-start.11 = (f32[128,32]{1,0:T(8,128)S(1)}, f32[128,32]{1,0:T(8,128)}, u32[]{:S(2)}) copy-start(f32[128,32]{1,0:T(8,128)} %copy.74) | copy-start | bytes 49156
  109.7 0.6 copy-start.13
  109.7 0.6 copy-start.14
  109.7 1.2 copy-start.4
  111.7 6.4 %copy-start.10 = (bf16[256,512]{1,0:T(8,128)(2,1)S(1)}, bf16[256,512]{1,0:T(8,128)(2,1)}, u32[]{:S(2)}) copy-start(bf16[256,512]{1,0:T(8,128)(2,1)} %param.16) | copy-start | bytes 786436
  116.8 3.8 %collective-permute-start.3 = (f32[2,128,576]{1,2,0:T(8,128)S(1)}, f32[2,128,576]{1,2,0:T(8,128)S(1)}, u32[]{:S(2)}, u32[]{:S(2)}) collective-permute-start(f32[2,128,576]{1,2,0:T(8,128)S(1)} %dynamic-slice_bitcast_fusion), channel_id=1, source_target_pairs={{0,1},{1,0},{2,3},{3,2},{4,5},{5,4},{6,7},{7,6},{8,9},{9,8},{10,11... | collective-permute-start | bytes 1769480 | tf_op jit(solution)/shard_map/ppermute | solution.py:83
  122.0 24.3 %copy-start.15 = (pred[512]{0:T(512)(128)(4,1)S(1)}, pred[512]{0:T(512)(128)(4,1)}, u32[]{:S(2)}) copy-start(pred[512]{0:T(512)(128)(4,1)} %get-tuple-element.87) | copy-start | bytes 1540
  122.0 24.3 %copy-start.16 = (pred[512]{0:T(512)(128)(4,1)S(1)}, pred[512]{0:T(512)(128)(4,1)}, u32[]{:S(2)}) copy-start(pred[512]{0:T(512)(128)(4,1)} %get-tuple-element.88) | copy-start | bytes 1540
  122.2 9.8 %collective-permute-start.4 = (f32[128,576]{1,0:T(8,128)S(1)}, f32[128,576]{1,0:T(8,128)S(1)}, u32[]{:S(2)}, u32[]{:S(2)}) collective-permute-start(f32[128,576]{1,0:T(8,128)S(1)} %bitcast.154), channel_id=1, source_target_pairs={{0,2},{2,0},{1,3},{3,1},{4,6},{6,4},{5,7},{7,5},{8,10},{10,8},{9,1... | collective-permute-start | bytes 884744 | tf_op jit(solution)/shard_map/ppermute | solution.py:83
  146.5 29.6 %copy-start.9 = (bf16[128,512]{1,0:T(8,128)(2,1)}, bf16[128,512]{1,0:T(8,128)(2,1)S(1)}, u32[]{:S(2)}) copy-start(bf16[128,512]{1,0:T(8,128)(2,1)S(1)} %fusion.25) | copy-start | bytes 393220
  186.5 4.6 %copy-start.7 = (bf16[512,4,128]{2,0,1:T(8,128)(2,1)S(1)}, bf16[512,4,128]{2,0,1:T(8,128)(2,1)}, u32[]{:S(2)}) copy-start(bf16[512,4,128]{2,0,1:T(8,128)(2,1)} %all_gather.22) | copy-start | bytes 1572868
  191.1 1.3 copy-start.12
Sparse Core Ops, SparseCore 0:
  11.3 15.5 all-gather.2
Sparse Core Ops, SparseCore 1:
  109.8 73.7 reduce-scatter.1
where the time goes:
time: 207 us
  matrix products  68.5 us (33%)
  blocking collectives  41.8 us (20%)
  waiting for transfers between devices  33.8 us (16%)
  local copies, waits for them, and re-layouts  22.2 us (11%)
  other arithmetic  18.4 us (9%)
  between operations  16.3 us (8%)
  starting transfers between devices  5.62 us (3%)
    dot_general x17, matrix products, product(): return jnp.dot(left, right, preferred_element_type=jnp.float32)  66.4 us
    ppermute x3, waiting for transfers between devices, shards(): following = lax.ppermute(held, 'tensor', shift) if step < ring - 1 else None  18.6 us
    all_gather x1, blocking collectives, shards(): kv_all = lax.all_gather(kv_local, 'tensor', axis=1, tiled=True)  15 us
    all_gather x1, blocking collectives, shards(): lax.all_gather(jnp.concatenate([low_query, low_keyval], axis=1), 'tensor'...  13.1 us
    all_gather x1, blocking collectives, shards(): lax.all_gather(jnp.concatenate([key_heads, value_heads], axis=1), ('seq',...  11.1 us
    ppermute x2, waiting for transfers between devices, ring_reduce_scatter(): total = lax.ppermute(total, axis, shift) + pick(step)  7.78 us
    reduce_scatter x1, waiting for transfers between devices, shards(): lax.psum_scatter(query_terms.reshape(ring * chunk, -1), ('seq', 'load'),...  7.43 us
    sub x1, other arithmetic, shards(): exp_scores = jnp.where(visible, jnp.exp(scores - row_top[..., None]), 0.0)  4.59 us
  transfers between devices with their start and end apart: 7, of which 5 were waited for; matrix products, arithmetic and copies ran while one was open for 45% of the time, Pallas kernels for 0%

commit v1 on v0

--- a/solution.py
+++ b/solution.py
@@ -10,6 +10,19 @@
 TENANTS = 4
 ROPE_BASE = 500000.0
 ADAPTER_ALPHA = 8.0
+
+
+def collect(array, axis, dim):
+    ways = lax.axis_size(axis)
+    up = [(d, (d + 1) % ways) for d in range(ways)]
+    down = [(d, (d - 1) % ways) for d in range(ways)]
+    earlier, later = ([array], [array])
+    for _ in range(ways // 2):
+        earlier.append(lax.ppermute(earlier[-1], axis, up))
+    for _ in range((ways - 1) // 2):
+        later.append(lax.ppermute(later[-1], axis, down))
+    line = jnp.concatenate([*earlier[::-1], *later[1:]], axis=dim)
+    return jnp.roll(line, (lax.axis_index(axis) - ways // 2) * array.shape[dim], axis=dim)
 
 
 def product(left, right):
@@ -192,9 +205,7 @@
     value_heads = lax.dynamic_slice_in_dim(
         kv_all, key_cols + kv_first * HEAD_DIM, kv_here * HEAD_DIM, 1
     ).reshape(block_rows, kv_here, HEAD_DIM)
-    both_heads = lax.all_gather(
-        jnp.concatenate([key_heads, value_heads], axis=1), ("seq", "load"), axis=0, tiled=True
-    )
+    both_heads = collect(jnp.concatenate([key_heads, value_heads], axis=1), ("seq", "load"), 0)
     piece_keys = both_heads[:, :kv_here]
     piece_values = both_heads[:, kv_here:]
     delta_query = lax.optimization_barrier(product(wide_query, up_query_all))

time: 207 us -> 213 us (1.029)
  blocking collectives: 41.8 us -> 31.2 us
  local copies, waits for them, and re-layouts: 22.2 us -> 29.9 us
  waiting for transfers between devices: 33.8 us -> 37 us
    all_gather x1 -> x0, blocking collectives: 11.1 us -> none  [shards(): lax.all_gather(jnp.concatenate([key_heads, value_heads], axis=1), ('seq',...]
    ppermute x0 -> x3, waiting for transfers between devices: none -> 10 us  [the longest x2 10 us: collect(): earlier.append(lax.ppermute(earlier[-1], axis, up))]
    reduce_scatter x1, waiting for transfers between devices: 7.43 us -> 0.01 us  [shards(): lax.psum_scatter(query_terms.reshape(ring * chunk, -1), ('seq', 'load'),...]
    unnamed x40 -> x43, local copies, waits for them, and re-layouts: 2.23 us -> 8.37 us
    unnamed x1 -> x3, other arithmetic: 4.37 us -> 5.72 us
  transfers between devices with their start and end apart: 7 -> 10, of which waited for: 5 -> 6; matrix products, arithmetic and copies ran while one was open for 45% -> 48% of each run, Pallas kernels for 0% -> 0%
where the time goes in v1:
time: 213 us
  matrix products  70.4 us (33%)
  waiting for transfers between devices  37 us (17%)
  blocking collectives  31.2 us (15%)
  local copies, waits for them, and re-layouts  29.9 us (14%)
  other arithmetic  20.4 us (10%)
  between operations  16.2 us (8%)
  starting transfers between devices  7.38 us (3%)
    dot_general x17, matrix products, product(): return jnp.dot(left, right, preferred_element_type=jnp.float32)  66.4 us
    ppermute x3, waiting for transfers between devices, shards(): following = lax.ppermute(held, 'tensor', shift) if step < ring - 1 else None  18.6 us
    all_gather x1, blocking collectives, shards(): kv_all = lax.all_gather(kv_local, 'tensor', axis=1, tiled=True)  15.5 us
    all_gather x1, blocking collectives, shards(): lax.all_gather(jnp.concatenate([low_query, low_keyval], axis=1), 'tensor'...  13.1 us
    ppermute x2, waiting for transfers between devices, collect(): earlier.append(lax.ppermute(earlier[-1], axis, up))  10 us
    ppermute x2, waiting for transfers between devices, ring_reduce_scatter(): total = lax.ppermute(total, axis, shift) + pick(step)  8.41 us
    unnamed x43, local copies, waits for them, and re-layouts  8.37 us
    unnamed x3, other arithmetic  5.72 us
  transfers between devices with their start and end apart: 10, of which 6 were waited for; matrix products, arithmetic and copies ran while one was open for 48% of the time, Pallas kernels for 0%

profile of v1, /device:TPU:0, one launch (start us, length us, event | category | flops | bytes accessed | tf_op | source)
XLA Modules:
  0.0 212.6 jit_solution(14028036621463900106)
XLA Ops:
  8.1 3.1 %collective-permute-start = (bf16[128,4096]{1,0:T(8,128)(2,1)}, bf16[128,4096]{1,0:T(8,128)(2,1)}, u32[]{:S(2)}, u32[]{:S(2)}) collective-permute-start(bf16[128,4096]{1,0:T(8,128)(2,1)} %param.10), channel_id=1, source_target_pairs={{0,4},{4,8},{8,12},{12,0},{1,5},{5,9},{9,13},{13,1},{2,6},{6,10},{... | collective-permute-start | bytes 3145736 | tf_op jit(solution)/shard_map/ppermute | solution.py:130
  11.4 0.8 reduce-window.8
  12.2 0.7 bitcast_subtract_fusion
  12.9 1.7 fusion.51
  14.7 0.5 fusion.52
  15.2 0.6 select_reduce_fusion.8
  16.1 2.9 %fusion.50 = f32[128,512]{1,0:T(8,128)S(1)} fusion(bf16[128,4096]{1,0:T(8,128)(2,1)S(1)} %copy-done.5, bf16[4096,512]{1,0:T(8,128)(2,1)} %param.12), kind=kOutput, calls=%fused_computation.156 | convolution fusion | flops 536870912 | bytes 5505024 | tf_op jit(solution)/shard_map/dot_general | solution.py:29
  19.3 1.1 broadcast_in_dim.269
  20.4 0.7 constant_dynamic-update-slice_fusion.11
  21.2 15.5 %collective-permute-done = bf16[128,4096]{1,0:T(8,128)(2,1)} collective-permute-done((bf16[128,4096]{1,0:T(8,128)(2,1)}, bf16[128,4096]{1,0:T(8,128)(2,1)}, u32[]{:S(2)}, u32[]{:S(2)}) %collective-permute-start) | collective-permute-done | bytes 1048608 | tf_op jit(solution)/shard_map/ppermute | solution.py:130
  36.7 1.7 fusion.54
  38.4 1.7 fusion.55
  40.2 2.8 %fusion.53 = f32[128,512]{1,0:T(8,128)} fusion(bf16[128,4096]{1,0:T(8,128)(2,1)} %collective-permute-done, bf16[4096,512]{1,0:T(8,128)(2,1)S(1)} %copy-done.1), kind=kOutput, calls=%fused_computation.159 | convolution fusion | flops 536870912 | bytes 5505024 | tf_op jit(solution)/shard_map/dot_general | solution.py:29
  43.2 0.7 copy.71
  43.9 1.1 maximum_bitcast_fusion.1
  45.0 0.9 copy.72
  45.9 15.3 %fusion.13 = f32[256,4096]{1,0:T(8,128)S(1)} fusion(bf16[4096,4096]{1,0:T(8,128)(2,1)} %param.11, bf16[128,4096]{1,0:T(8,128)(2,1)} %collective-permute-done, bf16[128,4096]{1,0:T(8,128)(2,1)S(1)} %copy-done.6), kind=kOutput, calls=%fused_computation.21 | convolution fusion | flops 8594128896 | bytes 39845888 | tf_op jit(solution)/shard_map/dot_general | solution.py:29
  61.2 4.3 %broadcast_in_dim.276 = f32[4,128,4096]{2,1,0:T(8,128)} broadcast(f32[]{:T(128)} %constant.212.clone.1), dimensions={} | broadcast | bytes 8388612 | tf_op jit(solution)/shard_map/broadcast_in_dim | solution.py:126
  65.5 1.5 fusion.12
  67.0 0.7 constant_dynamic-update-slice_fusion.10
  67.8 1.5 fusion.11
  69.4 1.2 collective-permute-start.2
  70.5 14.2 %fusion.3 = f32[4,128,4096]{2,1,0:T(8,128)} fusion(f32[4,128,4096]{2,1,0:T(8,128)} %fusion.11, s32[]{:T(128)S(6)} %select_n.276, bf16[128,4096]{1,0:T(8,128)(2,1)S(1)} %collective-permute-done.1, bf16[4096,4096]{1,0:T(8,128)(2,1)} %param.11), kind=kOutput, calls=%fused_computation.7 | convolution fusion | flops 4294967296 | bytes 36700164 | tf_op jit(solution)/shard_map/dot_general | solution.py:29
  84.8 0.5 fusion.57
  85.3 0.5 fusion.58
  86.1 0.7 copy.74
  86.8 2.9 %fusion.56 = f32[128,512]{1,0:T(8,128)S(1)} fusion(bf16[128,4096]{1,0:T(8,128)(2,1)S(1)} %collective-permute-done.1, bf16[4096,512]{1,0:T(8,128)(2,1)} %param.12), kind=kOutput, calls=%fused_computation.162 | convolution fusion | flops 536870912 | bytes 5505024 | tf_op jit(solution)/shard_map/dot_general | solution.py:29
  89.8 0.9 copy.75
  90.7 1.7 constant_dynamic-update-slice_fusion.9
  92.4 3.0 %collective-permute-done.2 = bf16[128,4096]{1,0:T(8,128)(2,1)S(1)} collective-permute-done((bf16[128,4096]{1,0:T(8,128)(2,1)S(1)}, bf16[128,4096]{1,0:T(8,128)(2,1)S(1)}, u32[]{:S(2)}, u32[]{:S(2)}) %collective-permute-start.2) | collective-permute-done | bytes 1048608 | tf_op jit(solution)/shard_map/ppermute | solution.py:130
  95.4 14.2 %fusion.2 = f32[4,128,4096]{2,1,0:T(8,128)} fusion(f32[4,128,4096]{2,1,0:T(8,128)} %fusion.3, s32[]{:T(128)S(6)} %select_n.281, bf16[128,4096]{1,0:T(8,128)(2,1)S(1)} %collective-permute-done.2, bf16[4096,4096]{1,0:T(8,128)(2,1)} %param.11), kind=kOutput, calls=%fused_computation.5 | convolution fusion | flops 4294967296 | bytes 36700164 | tf_op jit(solution)/shard_map/dot_general | solution.py:29
  109.7 0.5 copy-done.14
  110.3 0.5 fusion.60
  111.7 2.9 %fusion.59 = f32[128,512]{1,0:T(8,128)S(1)} fusion(bf16[128,4096]{1,0:T(8,128)(2,1)S(1)} %collective-permute-done.2, bf16[4096,512]{1,0:T(8,128)(2,1)} %param.12), kind=kOutput, calls=%fused_computation.165 | convolution fusion | flops 536870912 | bytes 5505024 | tf_op jit(solution)/shard_map/dot_general | solution.py:29
  114.9 0.7 constant_dynamic-update-slice_fusion.8
  115.7 1.2 dynamic-slice_bitcast_fusion
  117.0 1.2 negate_select_fusion.1
  118.2 2.6 %all_gather.17 = bf16[512,512]{1,0:T(8,128)(2,1)S(1)} all-gather(bf16[256,512]{1,0:T(8,128)(2,1)S(1)} %copy-done.9), channel_id=1, replica_groups=mesh['groups'=2,'tensor'=4,'seq'=2,'load'=2] {'load'}, dimensions={0}, use_global_device_ids=true | all-gather | bytes 786432 | tf_op jit(solution)/shard_map/all_gather | solution.py:121
  120.7 1.3 bitcast_add_fusion
  122.2 1.2 collective-permute-start.4
  123.6 8.4 %collective-permute-done.4 = f32[128,576]{1,0:T(8,128)S(1)} collective-permute-done((f32[128,576]{1,0:T(8,128)S(1)}, f32[128,576]{1,0:T(8,128)S(1)}, u32[]{:S(2)}, u32[]{:S(2)}) %collective-permute-start.4) | collective-permute-done | bytes 294944 | tf_op jit(solution)/shard_map/ppermute | solution.py:96
  132.4 13.1 %all-gather = bf16[128,256]{0,1:T(8,128)(2,1)S(1)} all-gather(bf16[128,64]{0,1:T(8,128)(2,1)S(1)} %copy.81), channel_id=2, replica_groups=mesh['groups'=2,'tensor'=4,'seq'=2,'load'=2] {'tensor'}, dimensions={1}, use_global_device_ids=true | all-gather | bytes 81920 | tf_op jit(solution)/shard_map/all_gather | solution.py:183
  146.5 15.5 %all_gather.18 = bf16[128,2048]{1,0:T(8,128)(2,1)S(1)} all-gather(bf16[128,512]{1,0:T(8,128)(2,1)S(1)} %fusion.25), channel_id=1, replica_groups=mesh['groups'=2,'tensor'=4,'seq'=2,'load'=2] {'tensor'}, dimensions={1}, use_global_device_ids=true | all-gather | bytes 655360 | tf_op jit(solution)/shard_map/all_gather | solution.py:195
  162.5 0.7 pad_maximum_fusion
  163.2 0.7 fusion.26
  163.9 1.7 collective-permute-start.7
  165.6 5.7 %collective-permute-done.5 = bf16[128,4,128]{2,0,1:T(8,128)(2,1)S(1)} collective-permute-done((bf16[128,4,128]{2,0,1:T(8,128)(2,1)}, bf16[128,4,128]{2,0,1:T(8,128)(2,1)S(1)}, u32[]{:S(2)}, u32[]{:S(2)}) %collective-permute-start.5) | collective-permute-done | bytes 131104 | tf_op jit(solution)/shard_map/ppermute | solution.py:21
  171.3 2.9 %fusion.62 = f32[128,4096]{1,0:T(8,128)S(1)} fusion(bf16[128,512]{0,1:T(8,128)(2,1)S(1)} %bitcast.152, bf16[512,4096]{1,0:T(8,128)(2,1)} %all-gather.3.cloned.1.call-done), kind=kOutput, calls=%fused_computation.168 | convolution fusion | flops 536870912 | bytes 6422528 | tf_op jit(solution)/shard_map/dot_general | solution.py:29
  174.3 4.3 %collective-permute-done.6 = bf16[128,4,128]{2,0,1:T(8,128)(2,1)} collective-permute-done((bf16[128,4,128]{2,0,1:T(8,128)(2,1)S(1)}, bf16[128,4,128]{2,0,1:T(8,128)(2,1)}, u32[]{:S(2)}, u32[]{:S(2)}) %collective-permute-start.6) | collective-permute-done | bytes 131104 | tf_op jit(solution)/shard_map/ppermute | solution.py:21
  178.6 1.6 constant_dynamic-update-slice_fusion.7
  180.2 0.7 constant_dynamic-update-slice_fusion.6
  180.8 0.7 constant_dynamic-update-slice_fusion.5
  181.5 1.6 constant_dynamic-update-slice_fusion.4
  183.1 1.6 constant_dynamic-update-slice_fusion.3
  184.7 0.7 constant_dynamic-update-slice_fusion.2
  185.4 0.7 constant_dynamic-update-slice_fusion.1
  186.1 1.6 constant_dynamic-update-slice_fusion
  187.6 1.8 add.327
  189.5 0.7 fusion.44
  190.6 4.4 %fusion.22 = bf16[16,8,32,128]{3,1,2,0:T(8,128)(2,1)S(1)} fusion(f32[16,8,32,128]{3,2,1,0:T(8,128)S(1)} %bitcast.148, f32[128,4095]{1,0:T(8,128)S(1)} %get-tuple-element.58, f32[128,1]{1,0:T(8,128)S(1)} %get-tuple-element.60, f32[128,1]{1,0:T(8,128)S(1)} %get-tuple-element.59, f32[128,4095]{1,0:T(8,128)S(1)} %get-tuple-element.57, f32[128,4096]{1,0:T(8,128)S(1)} %add.327, ...), kind=kLoop, calls=%fused_computation.30 | loop fusion | flops 3670016 | bytes 11538432
  195.2 2.3 %fusion.20 = f32[2,512,128,16]{2,1,3,0:T(8,128)S(1)} fusion(bf16[128,2,16,128]{3,2,1,0:T(8,128)(2,1)S(1)} %bitcast.146, bf16[1024,4,128]{2,0,1:T(8,128)(2,1)} %constant_dynamic-update-slice_fusion, s32[]{:T(128)S(6)} %select_n.307), kind=kOutput, calls=%fused_computation.28 | convolution fusion | flops 536870912 | bytes 9699332 | tf_op jit(solution)/shard_map/qghd,kgd->ghqk/dot_general | solution.py:218
  197.5 4.6 %fusion.49 = (f32[2,16,128]{2,1,0:T(8,128)S(1)}, bf16[2,16,128,512]{2,3,1,0:T(8,128)(2,1)S(1)}) fusion(f32[2,512,128,16]{2,1,3,0:T(8,128)S(1)} %fusion.20, pred[128,512]{0,1:T(8,128)(4,1)S(1)} %copy-done.13), kind=kOutput, calls=%fused_computation.155 | output fusion | flops 16777728 | bytes 12664832 | tf_op jit(solution)/shard_map/sub | solution.py:223
  202.1 1.7 fusion.17
  203.8 1.3 copy.89
  (103 shorter events, 5.2 us)
Async XLA Ops:
  8.0 4.9 %copy-start = (bf16[4096,128]{1,0:T(8,128)(2,1)S(1)}, bf16[4096,128]{1,0:T(8,128)(2,1)}, u32[]{:S(2)}) copy-start(bf16[4096,128]{1,0:T(8,128)(2,1)} %param.13) | copy-start | bytes 3145732
  8.0 6.6 %copy-start.5 = (bf16[128,4096]{1,0:T(8,128)(2,1)S(1)}, bf16[128,4096]{1,0:T(8,128)(2,1)}, u32[]{:S(2)}) copy-start(bf16[128,4096]{1,0:T(8,128)(2,1)} %param.10) | copy-start | bytes 3145732
  8.0 6.6 %copy-start.2 = (bf16[4096,128]{1,0:T(8,128)(2,1)S(1)}, bf16[4096,128]{1,0:T(8,128)(2,1)}, u32[]{:S(2)}) copy-start(bf16[4096,128]{1,0:T(8,128)(2,1)} %param.14) | copy-start | bytes 3145732
  8.0 7.2 %copy-start.16 = (s32[4]{0:T(128)S(1)}, s32[4]{0:T(128)}, u32[]{:S(2)}) copy-start(s32[4]{0:T(128)} %param.17) | copy-start | bytes 52
  8.0 7.2 %copy-start.17 = (s32[4]{0:T(128)S(1)}, s32[4]{0:T(128)}, u32[]{:S(2)}) copy-start(s32[4]{0:T(128)} %param.19) | copy-start | bytes 52
  8.1 163.3 %all-gather.3.cloned.1.call-start = ((), (), s32[]{:S(2)}) async-start(), calls=%async_computation.2 | async-start | bytes 6291456 | tf_op jit(solution)/shard_map/all_gather | solution.py:120
  8.1 28.6 %collective-permute-start = (bf16[128,4096]{1,0:T(8,128)(2,1)}, bf16[128,4096]{1,0:T(8,128)(2,1)}, u32[]{:S(2)}, u32[]{:S(2)}) collective-permute-start(bf16[128,4096]{1,0:T(8,128)(2,1)} %param.10), channel_id=1, source_target_pairs={{0,4},{4,8},{8,12},{12,0},{1,5},{5,9},{9,13},{13,1},{2,6},{6,10},{... | collective-permute-start | bytes 3145736 | tf_op jit(solution)/shard_map/ppermute | solution.py:130
  11.2 176.4 %reduce-scatter.2.cloned.1.call-start = ((), (), s32[]{:S(2)}) async-start(), calls=%async_computation.1 | async-start | bytes 10485760 | tf_op jit(solution)/shard_map/reduce_scatter | solution.py:170
  19.3 20.9 %copy-start.1 = (bf16[4096,512]{1,0:T(8,128)(2,1)S(1)}, bf16[4096,512]{1,0:T(8,128)(2,1)}, u32[]{:S(2)}) copy-start(bf16[4096,512]{1,0:T(8,128)(2,1)} %param.12) | copy-start | bytes 12582916
  40.2 5.7 %copy-start.6 = (bf16[128,4096]{1,0:T(8,128)(2,1)S(1)}, bf16[128,4096]{1,0:T(8,128)(2,1)}, u32[]{:S(2)}) copy-start(bf16[128,4096]{1,0:T(8,128)(2,1)} %param.10) | copy-start | bytes 3145732
  43.0 26.4 %collective-permute-start.1 = (bf16[128,4096]{1,0:T(8,128)(2,1)}, bf16[128,4096]{1,0:T(8,128)(2,1)S(1)}, u32[]{:S(2)}, u32[]{:S(2)}) collective-permute-start(bf16[128,4096]{1,0:T(8,128)(2,1)} %collective-permute-done), channel_id=1, source_target_pairs={{0,4},{4,8},{8,12},{12,0},{1,5},{5,9},{9,13},{13,1},{2,6},{6,10},{... | collective-permute-start | bytes 3145736 | tf_op jit(solution)/shard_map/ppermute | solution.py:130
  65.5 1.5 copy-start.7
  69.3 16.0 %copy-start.3 = (bf16[4096,128]{1,0:T(8,128)(2,1)S(1)}, bf16[4096,128]{1,0:T(8,128)(2,1)}, u32[]{:S(2)}) copy-start(bf16[4096,128]{1,0:T(8,128)(2,1)} %param.14) | copy-start | bytes 3145732
  69.4 26.1 %collective-permute-start.2 = (bf16[128,4096]{1,0:T(8,128)(2,1)S(1)}, bf16[128,4096]{1,0:T(8,128)(2,1)S(1)}, u32[]{:S(2)}, u32[]{:S(2)}) collective-permute-start(bf16[128,4096]{1,0:T(8,128)(2,1)S(1)} %collective-permute-done.1), channel_id=1, source_target_pairs={{0,4},{4,8},{8,12},{12,0},{1,5},{5,9},{9,13},{13,1},{2,6},{6,10},{... | collective-permute-start | bytes 3145736 | tf_op jit(solution)/shard_map/ppermute | solution.py:130
  86.8 2.9 %copy-start.12 = (f32[128,32]{1,0:T(8,128)S(1)}, f32[128,32]{1,0:T(8,128)}, u32[]{:S(2)}) copy-start(f32[128,32]{1,0:T(8,128)} %copy.74) | copy-start | bytes 49156
  109.7 0.6 copy-start.14
  109.7 0.6 copy-start.15
  109.7 1.2 copy-start.4
  111.7 6.5 %copy-start.9 = (bf16[256,512]{1,0:T(8,128)(2,1)S(1)}, bf16[256,512]{1,0:T(8,128)(2,1)}, u32[]{:S(2)}) copy-start(bf16[256,512]{1,0:T(8,128)(2,1)} %param.16) | copy-start | bytes 786436
  116.8 3.9 %collective-permute-start.3 = (f32[2,128,576]{1,2,0:T(8,128)S(1)}, f32[2,128,576]{1,2,0:T(8,128)S(1)}, u32[]{:S(2)}, u32[]{:S(2)}) collective-permute-start(f32[2,128,576]{1,2,0:T(8,128)S(1)} %dynamic-slice_bitcast_fusion), channel_id=1, source_target_pairs={{0,1},{1,0},{2,3},{3,2},{4,5},{5,4},{6,7},{7,6},{8,9},{9,8},{10,11... | collective-permute-start | bytes 1769480 | tf_op jit(solution)/shard_map/ppermute | solution.py:96
  122.2 9.8 %collective-permute-start.4 = (f32[128,576]{1,0:T(8,128)S(1)}, f32[128,576]{1,0:T(8,128)S(1)}, u32[]{:S(2)}, u32[]{:S(2)}) collective-permute-start(f32[128,576]{1,0:T(8,128)S(1)} %bitcast.154), channel_id=1, source_target_pairs={{0,2},{2,0},{1,3},{3,1},{4,6},{6,4},{5,7},{7,5},{8,10},{10,8},{9,1... | collective-permute-start | bytes 884744 | tf_op jit(solution)/shard_map/ppermute | solution.py:96
  146.5 15.6 %copy-start.8 = (bf16[128,512]{1,0:T(8,128)(2,1)}, bf16[128,512]{1,0:T(8,128)(2,1)S(1)}, u32[]{:S(2)}) copy-start(bf16[128,512]{1,0:T(8,128)(2,1)S(1)} %fusion.25) | copy-start | bytes 393220
  163.2 8.1 %collective-permute-start.5 = (bf16[128,4,128]{2,0,1:T(8,128)(2,1)}, bf16[128,4,128]{2,0,1:T(8,128)(2,1)S(1)}, u32[]{:S(2)}, u32[]{:S(2)}) collective-permute-start(bf16[128,4,128]{2,0,1:T(8,128)(2,1)} %pad_maximum_fusion), channel_id=1, source_target_pairs={{0,1},{1,2},{2,3},{3,0},{4,5},{5,6},{6,7},{7,4},{8,9},{9,10},{10,1... | collective-permute-start | bytes 393224 | tf_op jit(solution)/shard_map/ppermute | solution.py:21
  163.9 17.6 %collective-permute-start.7 = (bf16[128,4,128]{2,0,1:T(8,128)(2,1)}, bf16[128,4,128]{2,0,1:T(8,128)(2,1)}, u32[]{:S(2)}, u32[]{:S(2)}) collective-permute-start(bf16[128,4,128]{2,0,1:T(8,128)(2,1)} %pad_maximum_fusion), channel_id=1, source_target_pairs={{0,3},{1,0},{2,1},{3,2},{4,7},{5,4},{6,5},{7,6},{8,11},{9,8},{10,9... | collective-permute-start | bytes 393224 | tf_op jit(solution)/shard_map/ppermute | solution.py:23
  171.3 7.3 %collective-permute-start.6 = (bf16[128,4,128]{2,0,1:T(8,128)(2,1)S(1)}, bf16[128,4,128]{2,0,1:T(8,128)(2,1)}, u32[]{:S(2)}, u32[]{:S(2)}) collective-permute-start(bf16[128,4,128]{2,0,1:T(8,128)(2,1)S(1)} %collective-permute-done.5), channel_id=1, source_target_pairs={{0,1},{1,2},{2,3},{3,0},{4,5},{5,6},{6,7},{7,4},{8,9},{9,10},{10,1... | collective-permute-start | bytes 393224 | tf_op jit(solution)/shard_map/ppermute | solution.py:21
  189.5 0.8 copy-start.11
  189.5 1.0 copy-start.10
  195.2 2.3 %copy-start.13 = (pred[128,512]{0,1:T(8,128)(4,1)S(1)}, pred[128,512]{0,1:T(8,128)(4,1)}, u32[]{:S(2)}) copy-start(pred[128,512]{0,1:T(8,128)(4,1)} %fusion.26) | copy-start | bytes 196612
Sparse Core Ops, SparseCore 0:
  11.3 15.5 all-gather.2
Sparse Core Ops, SparseCore 1:
  109.8 75.2 reduce-scatter.1
